TPU v7x, 128 devices: a whole 4x4x4 slice. The times are simulated.
128 devices in a mesh: wide: 32 (over x, y, core), narrow: 4 (over z).
Axes of the slice: x: 4, y: 4, z: 4, core: 2. Of those that a mesh axis runs over, the one named last changes fastest.
Arguments:
- raw_samples: bfloat16 [1024, 32, 16384], P(('wide', 'narrow')), as said below
- filter_taps: float32 [64], replicated, may hold values from -0.75 to 0.75
- tile_pairs: int32 [16, 2], replicated, may hold values from 0 to 127, as said below
- tile_owners: int32 [16], replicated, may hold values from 0 to 3, as said below
Outputs:
- correlation_stacks: float32 [32, 64, 512], P('narrow', 'wide')
Inputs may be any that keep to these rules, and one draw needn't show every extreme that they name: `raw_samples`: noise samples, scaled per channel and per window. `tile_pairs`: each row is (source block, receiver block), and the two blocks differ. `tile_owners`: each owner has at most 8 tiles, and some owner has exactly 8.
All inputs are finite; a program needn't handle non-finite values.
Results may differ from a plain program's by a relative error of at most 0.0074.
Values may be sent and summed in bfloat16 or wider, within the bound.
No kernel may reach another device: no remote copies, remote signals or barrier semaphores. Data moves between devices by JAX's collectives and lax.ppermute only.
A program may use at most 128 MiB of HBM per device.

v0:
```python
import math
import jax
import jax.numpy as jnp
from jax import lax
from jax.sharding import PartitionSpec as P

NFFT = 4096
DECIM = 4
NBINS = 1024
SMOOTH = 63
LAGS = 512
BLK = 8
SLOTS = 8
water_level = 0.2
epsilon = 1e-06


def fir_tables(filter_taps, block_size):
    in_rows = jnp.arange(DECIM * block_size, dtype=jnp.int32)[:, None]
    out_cols = jnp.arange(block_size, dtype=jnp.int32)[None, :]
    this_index = DECIM * out_cols + DECIM - 1 - in_rows
    last_index = this_index + DECIM * block_size
    tap_count = filter_taps.shape[0]

    def taps_at(tap_index):
        inside = (tap_index >= 0) & (tap_index < tap_count)
        values = jnp.take(filter_taps, jnp.clip(tap_index, 0, tap_count - 1))
        return jnp.where(inside, values, jnp.zeros_like(values)).astype(jnp.bfloat16)

    return (taps_at(this_index), taps_at(last_index))


def decimate(samples, filter_taps):
    row_count, row_length = samples.shape
    block_size = min(128, row_length // DECIM)
    this_table, last_table = fir_tables(filter_taps, block_size)
    segments = samples.reshape(-1, DECIM * block_size)
    current = jnp.dot(segments, this_table, preferred_element_type=jnp.float32).reshape(
        row_count, -1, block_size
    )
    spilled = jnp.dot(segments, last_table, preferred_element_type=jnp.float32).reshape(
        row_count, -1, block_size
    )
    spilled = jnp.pad(spilled[:, :-1], ((0, 0), (1, 0), (0, 0)))
    return (current + spilled).reshape(row_count, -1).astype(jnp.bfloat16)


def dft_table(point_count, bin_count):
    sample_index = jnp.arange(point_count, dtype=jnp.int32)[:, None]
    frequency = 1 + jnp.arange(bin_count, dtype=jnp.int32)[None, :]
    angle = (sample_index * frequency % point_count).astype(jnp.float32) * (
        2.0 * math.pi / point_count
    )
    return jnp.concatenate([jnp.cos(angle), -jnp.sin(angle)], axis=1).astype(jnp.bfloat16)


def lag_table(point_count, bin_count, lag_count, window_count):
    frequency = 1 + jnp.arange(bin_count, dtype=jnp.int32)[:, None]
    shifted = jnp.arange(lag_count, dtype=jnp.int32)[None, :] - lag_count // 2 + point_count
    angle = (frequency * shifted % point_count).astype(jnp.float32) * (2.0 * math.pi / point_count)
    weight = 1.0 / math.sqrt(window_count * bin_count)
    return jnp.concatenate([jnp.cos(angle) * weight, -jnp.sin(angle) * weight], axis=0)


def smoother(bin_count, span_width):
    bin_index = jnp.arange(bin_count, dtype=jnp.int32)
    nearby = (jnp.abs(bin_index[:, None] - bin_index[None, :]) <= (span_width - 1) // 2).astype(
        jnp.float32
    )
    return nearby / jnp.sum(nearby, axis=0, keepdims=True)


def whiten(decimated):
    spectrum = jnp.dot(
        decimated, dft_table(decimated.shape[1], NBINS), preferred_element_type=jnp.float32
    )
    real_part = spectrum[:, :NBINS]
    imag_part = spectrum[:, NBINS:]
    magnitude = jnp.sqrt(real_part * real_part + imag_part * imag_part)
    smooth = jnp.dot(magnitude, smoother(NBINS, SMOOTH), precision=lax.Precision.HIGHEST)
    floor_level = water_level * jnp.mean(smooth, axis=1, keepdims=True) + epsilon
    factor = 1.0 / (smooth + floor_level)
    return (spectrum * jnp.concatenate([factor, factor], axis=1)).astype(jnp.bfloat16)


def block_start(block_index, chan_dev, wide_count, narrow_count):
    first_channel = block_index * BLK
    shard_index = first_channel // chan_dev
    return (
        shard_index % narrow_count * wide_count + shard_index // narrow_count
    ) * chan_dev + first_channel % chan_dev


def gather_rows(spectra, starts):

    def one_block(start_row):
        return lax.dynamic_slice_in_dim(spectra, start_row, BLK, 0)

    return jax.vmap(one_block)(starts)


def slot_cross(source, target, live_slots):
    highest = lax.Precision.HIGHEST
    src_real = source[..., :NBINS]
    src_imag = source[..., NBINS:]
    dst_real = target[..., :NBINS]
    dst_imag = target[..., NBINS:]
    real_sum = jnp.einsum("siwf,sjwf->ijsf", src_real, dst_real, precision=highest) + jnp.einsum(
        "siwf,sjwf->ijsf", src_imag, dst_imag, precision=highest
    )
    imag_sum = jnp.einsum("siwf,sjwf->ijsf", src_real, dst_imag, precision=highest) - jnp.einsum(
        "siwf,sjwf->ijsf", src_imag, dst_real, precision=highest
    )
    slot_count = source.shape[0]
    merged = jnp.concatenate(
        [
            real_sum.reshape(BLK * BLK, slot_count, NBINS),
            imag_sum.reshape(BLK * BLK, slot_count, NBINS),
        ],
        axis=2,
    )
    return merged * live_slots[None, :, None]


def stack_pairs(partial_value, window_count, wide_count):
    lag_basis = lag_table(NFFT, NBINS, LAGS, window_count)
    slot_count = partial_value.shape[1]
    pair_share = partial_value.shape[0] // wide_count
    summed = lax.psum_scatter(partial_value, "wide", scatter_dimension=0, tiled=True)
    flat = summed.reshape(pair_share * slot_count, 2 * NBINS)
    return jnp.dot(flat, lag_basis, precision=lax.Precision.HIGHEST).reshape(
        pair_share, slot_count, LAGS
    )


def on_device(raw_samples, filter_taps, tile_pairs, tile_owners):
    wide_count = lax.axis_size("wide")
    narrow_count = lax.axis_size("narrow")
    chan_dev = raw_samples.shape[0]
    window_total = raw_samples.shape[1]
    arrived = lax.all_to_all(raw_samples, "wide", split_axis=1, concat_axis=0, tiled=True)
    flat_rows = arrived.reshape(-1, arrived.shape[2])
    whitened = whiten(decimate(flat_rows, filter_taps)).reshape(
        arrived.shape[0], arrived.shape[1], 2 * NBINS
    )
    owner_index = lax.axis_index("narrow")
    slot_ids = jnp.arange(SLOTS, dtype=jnp.int32)
    owner_ids = jnp.arange(narrow_count, dtype=jnp.int32)
    owned_all = tile_owners[None, :] == owner_ids[:, None]
    rank_all = jnp.cumsum(owned_all.astype(jnp.int32), axis=1) - 1
    select_all = owned_all[:, None, :] & (rank_all[:, None, :] == slot_ids[None, :, None])
    select = lax.dynamic_index_in_dim(select_all, owner_index, 0, keepdims=False)
    pick_all = select_all.astype(jnp.int32)
    chosen_all = jnp.sum(pick_all[:, :, :, None] * tile_pairs[None, None, :, :], axis=2)
    chosen = lax.dynamic_index_in_dim(chosen_all, owner_index, 0, keepdims=False)
    live_slots = jnp.sum(select.astype(jnp.int32), axis=1).astype(jnp.float32)
    spectra = lax.all_gather(whitened, "narrow", axis=0, tiled=True)
    source = gather_rows(
        spectra, block_start(chosen[:, 0], chan_dev, wide_count, narrow_count)
    ).astype(jnp.float32)
    target = gather_rows(
        spectra, block_start(chosen[:, 1], chan_dev, wide_count, narrow_count)
    ).astype(jnp.float32)
    partial_value = slot_cross(source, target, live_slots)
    stacked = jnp.transpose(stack_pairs(partial_value, window_total, wide_count), (1, 0, 2))
    return stacked


def solution(mesh):
    in_specs = (P(("wide", "narrow"), None, None), P(), P(), P())
    out_specs = P("narrow", "wide", None)
    return jax.shard_map(
        on_device, mesh=mesh, in_specs=in_specs, out_specs=out_specs, check_vma=False
    )
```

profile of v0, /device:TPU:0, one launch (start us, length us, event | category | flops | bytes accessed | tf_op | source)
XLA Modules:
  0.0 474.6 jit_solution(13282219317979138211)
XLA Ops:
  6.5 11.2 %copy.33 = bf16[8,32,16384]{2,0,1:T(8,128)(2,1)} copy(bf16[8,32,16384]{2,1,0:T(8,128)(2,1)} %param.6) | data formatting | bytes 16777216 | tf_op args[0]
  17.7 7.7 %all-to-all-start = ((bf16[8,32,16384]{2,0,1:T(8,128)(2,1)}), bf16[8,32,16384]{2,0,1:T(8,128)(2,1)}, u32[]{:S(2)}, u32[]{:S(2)}) async-start(bf16[8,32,16384]{2,0,1:T(8,128)(2,1)} %copy.33), calls=%async_computation | async-start | bytes 16777216 | tf_op jit(solution)/shard_map/all_to_all | solution.py:141
  25.9 0.7 fusion.579
  26.6 0.7 fusion.580
  27.3 0.7 fusion.581
  28.1 0.7 fusion.582
  28.8 69.1 %cosine_convert_fusion = (bf16[4096,1024]{1,0:T(8,128)(2,1)}, bf16[4096,1024]{1,0:T(8,128)(2,1)}) fusion(s32[1024]{0:T(1024)S(1)} %iota_add_fusion), kind=kLoop, calls=%fused_computation.15 | loop fusion | flops 71303168 | bytes 16781312 | tf_op jit(solution)/shard_map/convert.24
  97.9 41.1 %all-to-all-done = bf16[8,32,16384]{2,0,1:T(8,128)(2,1)} async-done(((bf16[8,32,16384]{2,0,1:T(8,128)(2,1)}), bf16[8,32,16384]{2,0,1:T(8,128)(2,1)}, u32[]{:S(2)}, u32[]{:S(2)}) %all-to-all-start) | async-done | bytes 8388640 | tf_op jit(solution)/shard_map/all_to_all | solution.py:141
  138.9 13.5 %reshape_reshape.3 = bf16[8192,512]{1,0:T(8,128)(2,1)} reshape(bf16[32,8,1,16384]{3,1,0,2:T(8,128)(2,1)} %bitcast.65) | data formatting | bytes 16777216 | tf_op jit(solution)/shard_map/reshape;reshape | solution.py:37
  152.4 50.3 %convolution_bitcast_fusion = f32[8192,128]{0,1:T(8,128)} fusion(bf16[8192,512]{1,0:T(8,128)(2,1)} %reshape_reshape.3, bf16[]{:T(256)} %bitcast.63, bf16[]{:T(256)} %bitcast.62, bf16[]{:T(256)} %bitcast.61, bf16[]{:T(256)} %bitcast.60, bf16[]{:T(256)} %bitcast.59, bf16[]{:T(256)} %bitcast.58, bf16[]{:T(256)} %bitcast.57, bf16[]{:T(256)} %bitcast.56, ...), kind=kOutput, calls=%fused_computation.19 | convolution fusion | flops 1082916864 | bytes 12583552 | tf_op jit(solution)/shard_map/dot_general | solution.py:41
  202.7 45.8 %convolution_bitcast_fusion.1 = f32[8192,128]{0,1:T(8,128)} fusion(bf16[8192,512]{1,0:T(8,128)(2,1)S(1)} %bitcast.200, bf16[]{:T(256)} %bitcast.63, bf16[]{:T(256)} %bitcast.62, bf16[]{:T(256)} %bitcast.61, bf16[]{:T(256)} %bitcast.60, bf16[]{:T(256)} %bitcast.59, bf16[]{:T(256)} %bitcast.58, bf16[]{:T(256)} %bitcast.57, bf16[]{:T(256)} %bitcast.56, ...), kind=kOutput, calls=%fused_computation.20 | convolution fusion | flops 1082851328 | bytes 12583552 | tf_op jit(solution)/shard_map/dot_general | solution.py:38
  248.5 5.6 %copy.35 = f32[8192,128]{1,0:T(8,128)} copy(f32[8192,128]{0,1:T(8,128)} %convolution_bitcast_fusion) | data formatting | bytes 8388608 | tf_op jit(solution)/shard_map/dot_general | solution.py:41
  254.1 5.6 %copy.34 = f32[8192,128]{1,0:T(8,128)} copy(f32[8192,128]{0,1:T(8,128)} %convolution_bitcast_fusion.1) | data formatting | bytes 8388608 | tf_op jit(solution)/shard_map/dot_general | solution.py:38
  259.7 4.2 add_convert_fusion
  263.9 2.8 copy.36
  266.7 10.9 %fusion.3 = f32[256,2048]{1,0:T(8,128)S(1)} fusion(bf16[256,4096]{0,1:T(8,128)(2,1)} %bitcast.203, bf16[4096,1024]{1,0:T(8,128)(2,1)} %get-tuple-element.55, bf16[4096,1024]{1,0:T(8,128)(2,1)} %get-tuple-element.54), kind=kOutput, calls=%fused_computation.10 | convolution fusion | flops 4328521728 | bytes 20971520 | tf_op jit(solution)/shard_map/dot_general | solution.py:74
  277.6 3.8 fusion.583
  281.7 1.3 fusion.17
  283.7 57.0 %all-gather.3.cloned.1.call-done = bf16[1024,2048]{1,0:T(8,128)(2,1)} async-done(((bf16[256,2048]{1,0:T(8,128)(2,1)}), bf16[1024,2048]{1,0:T(8,128)(2,1)}) %all-gather.3.cloned.1.call-update) | async-done | bytes 4194320 | tf_op jit(solution)/shard_map/all_gather | solution.py:157
  340.7 18.2 %while.2 = (s32[]{:T(128)}, bf16[1024,1,2048]{2,0,1:T(8,128)(2,1)}, s32[8,3]{0,1:T(4,128)S(1)}, bf16[8,8,1,2048]{3,1,2,0:T(8,128)(2,1)S(1)}, s32[]{:T(128)}) while((s32[]{:T(128)}, bf16[1024,1,2048]{2,0,1:T(8,128)(2,1)}, s32[8,3]{0,1:T(4,128)S(1)}, bf16[8,8,1,2048]{3,1,2,0:T(8,128)(2,1)S(1)}, s32[]{:T(128)}) %tuple.109), condition=%wide.while_cond, body=%wide.while_body.sunk | while | flops 2 | bytes 65641 | solution.py:97
  341.0 0.6 slice.413
  341.6 1.5 bitcast_dynamic-update-slice_fusion.4
  343.3 0.6 slice.413
  343.9 1.5 bitcast_dynamic-update-slice_fusion.4
  345.5 0.6 slice.413
  346.1 1.5 bitcast_dynamic-update-slice_fusion.4
  347.8 0.6 slice.413
  348.4 1.5 bitcast_dynamic-update-slice_fusion.4
  350.0 0.6 slice.413
  350.6 1.5 bitcast_dynamic-update-slice_fusion.4
  352.8 1.5 bitcast_dynamic-update-slice_fusion.4
  355.1 1.5 bitcast_dynamic-update-slice_fusion.4
  357.3 1.5 bitcast_dynamic-update-slice_fusion.4
  359.3 17.9 %while.3 = (s32[]{:T(128)}, bf16[1024,1,2048]{2,0,1:T(8,128)(2,1)}, s32[8,3]{0,1:T(4,128)S(1)}, bf16[8,8,1,2048]{3,1,2,0:T(8,128)(2,1)S(1)}, s32[]{:T(128)}) while((s32[]{:T(128)}, bf16[1024,1,2048]{2,0,1:T(8,128)(2,1)}, s32[8,3]{0,1:T(4,128)S(1)}, bf16[8,8,1,2048]{3,1,2,0:T(8,128)(2,1)S(1)}, s32[]{:T(128)}) %tuple.110), condition=%wide.while_cond.1, body=%wide.while_body.1.sunk | while | flops 2 | bytes 65641 | solution.py:97
  360.0 1.5 bitcast_dynamic-update-slice_fusion.5
  362.2 1.5 bitcast_dynamic-update-slice_fusion.5
  363.8 0.6 slice.414
  364.4 1.5 bitcast_dynamic-update-slice_fusion.5
  366.7 1.5 bitcast_dynamic-update-slice_fusion.5
  368.9 1.5 bitcast_dynamic-update-slice_fusion.5
  371.1 1.5 bitcast_dynamic-update-slice_fusion.5
  373.4 1.5 bitcast_dynamic-update-slice_fusion.5
  375.6 1.5 bitcast_dynamic-update-slice_fusion.5
  378.1 2.6 maximum_multiply_fusion
  380.8 9.7 %cosine_multiply_fusion = (f32[1024,512]{1,0:T(8,128)S(1)}, f32[1024,512]{1,0:T(8,128)}) fusion(s32[512]{0:T(512)S(1)} %iota_add_fusion.1, s32[1024]{0:T(1024)S(1)} %iota_add_fusion), kind=kLoop, calls=%fused_computation.42 | loop fusion | flops 8912896 | bytes 4200448 | tf_op jit(solution)/shard_map/mul | solution.py:62
  390.5 72.8 %reduce-scatter.2.cloned.1.call-done = f32[2,8,2048]{2,1,0:T(8,128)} async-done(((f32[64,8,2048]{2,1,0:T(8,128)}), f32[2,8,2048]{2,1,0:T(8,128)}) %reduce-scatter.2.cloned.1.call-update) | async-done | bytes 131088 | tf_op jit(solution)/shard_map/reduce_scatter | solution.py:129
  463.3 3.8 fusion.20
  467.1 0.6 copy.41
  (67 shorter events, 9.9 us)
Async XLA Ops:
  17.7 8.1 %copy-start = (f32[64]{0:T(128)S(1)}, f32[64]{0:T(128)}, u32[]{:S(2)}) copy-start(f32[64]{0:T(128)} %param.7) | copy-start | bytes 772
  17.7 121.2 %all-to-all-start = ((bf16[8,32,16384]{2,0,1:T(8,128)(2,1)}), bf16[8,32,16384]{2,0,1:T(8,128)(2,1)}, u32[]{:S(2)}, u32[]{:S(2)}) async-start(bf16[8,32,16384]{2,0,1:T(8,128)(2,1)} %copy.33), calls=%async_computation | async-start | bytes 16777216 | tf_op jit(solution)/shard_map/all_to_all | solution.py:141
  25.4 315.2 %all-gather.3.cloned.1.call-start = ((), (), s32[]{:S(2)}) async-start(), calls=%async_computation.3 | async-start | bytes 5242880 | tf_op jit(solution)/shard_map/all_gather | solution.py:157
  152.4 50.3 %slice-start = ((s8[8388608]{0:T(1024)(128)(4,1)}), s8[4194304]{0:T(1024)(128)(4,1)S(1)}, s32[]{:S(2)}) async-start(s8[8388608]{0:T(1024)(128)(4,1)} %bitcast.199), calls=%async_computation.4 | async-start | bytes 8388608
  152.4 50.3 %slice-start.1 = ((s8[8388608]{0:T(1024)(128)(4,1)}), s8[4194304]{0:T(1024)(128)(4,1)S(1)}, s32[]{:S(2)}) async-start(s8[8388608]{0:T(1024)(128)(4,1)} %bitcast.199), calls=%async_computation.5 | async-start | bytes 8388608
  281.4 1.6 copy-start.2
  281.4 1.8 copy-start.1
  283.0 180.3 %reduce-scatter.2.cloned.1.call-start = ((), (), s32[]{:S(2)}) async-start(), calls=%async_computation.2 | async-start | bytes 4325376 | tf_op jit(solution)/shard_map/reduce_scatter | solution.py:129
Sparse Core Ops, SparseCore 0:
  283.1 57.5 all-gather.2
  380.9 82.3 reduce-scatter.1
where the time goes:
time: 477 us; the launch traced here: 475 us
  waiting for transfers between devices  171 us (36%)
  matrix products  115 us (24%)
  other arithmetic  88.6 us (19%)
  local copies, waits for them, and re-layouts  78.4 us (16%)
  between operations  13.6 us (3%)
  starting transfers between devices  7.96 us (2%)
    reduce_scatter x1, waiting for transfers between devices, stack_pairs(): lax.psum_scatter(partial_value, 'wide', scatter_dimension=0, tiled=True)  72.8 us
    another operation x3, other arithmetic  69.2 us
    all_gather x1, waiting for transfers between devices, on_device(): spectra = lax.all_gather(whitened, 'narrow', axis=0, tiled=True)  57 us
    dot_general x1, matrix products, decimate(): jnp.dot(segments, last_table, preferred_element_type=jnp.float32)  50.3 us
    dot_general x1, matrix products, decimate(): jnp.dot(segments, this_table, preferred_element_type=jnp.float32)  45.8 us
    all_to_all x1, waiting for transfers between devices, on_device(): lax.all_to_all(raw_samples, 'wide', split_axis=1, concat_axis=0, tiled=True)  41.1 us
    gather x48, local copies, waits for them, and re-layouts  35.5 us
    another operation x1, local copies, waits for them, and re-layouts, decimate(): segments = samples.reshape(-1, DECIM * block_size)  13.5 us
  transfers between devices with their start and end apart: 3, of which 3 were waited for; matrix products, arithmetic and copies ran while one was open for 17% of the time, Pallas kernels for 0%

commit v1 on v0

--- a/solution.py
+++ b/solution.py
@@ -154,7 +154,9 @@
     chosen_all = jnp.sum(pick_all[:, :, :, None] * tile_pairs[None, None, :, :], axis=2)
     chosen = lax.dynamic_index_in_dim(chosen_all, owner_index, 0, keepdims=False)
     live_slots = jnp.sum(select.astype(jnp.int32), axis=1).astype(jnp.float32)
-    spectra = lax.all_gather(whitened, "narrow", axis=0, tiled=True)
+    spectra = jnp.concatenate(
+        lax.all_to_all(jnp.stack(lax.axis_size("narrow") * [whitened]), "narrow", 0, 0), axis=0
+    )
     source = gather_rows(
         spectra, block_start(chosen[:, 0], chan_dev, wide_count, narrow_count)
     ).astype(jnp.float32)

time: 477 us -> 483 us (1.013)
  starting transfers between devices: 7.96 us -> 13.3 us
    all_gather x1 -> x0, waiting for transfers between devices: 57 us -> none  [on_device(): spectra = lax.all_gather(whitened, 'narrow', axis=0, tiled=True)]
    all_to_all x0 -> x1, waiting for transfers between devices: none -> 39.6 us  [on_device(): lax.all_to_all(jnp.stack(lax.axis_size('narrow') * [whitened]), 'narrow',...]
    reduce_scatter x1, waiting for transfers between devices: 72.8 us -> 91.8 us  [stack_pairs(): lax.psum_scatter(partial_value, 'wide', scatter_dimension=0, tiled=True)]
    all_to_all x0 -> x1, starting transfers between devices: none -> 5.44 us  [on_device(): lax.all_to_all(jnp.stack(lax.axis_size('narrow') * [whitened]), 'narrow',...]
where the time goes in v1:
time: 483 us; the launch traced here: 480 us
  waiting for transfers between devices  173 us (36%)
  matrix products  114 us (24%)
  other arithmetic  87.7 us (18%)
  local copies, waits for them, and re-layouts  77.8 us (16%)
  between operations  13.6 us (3%)
  starting transfers between devices  13.3 us (3%)
    reduce_scatter x1, waiting for transfers between devices, stack_pairs(): lax.psum_scatter(partial_value, 'wide', scatter_dimension=0, tiled=True)  91.8 us
    another operation x3, other arithmetic  69.2 us
    dot_general x1, matrix products, decimate(): jnp.dot(segments, last_table, preferred_element_type=jnp.float32)  50.2 us
    dot_general x1, matrix products, decimate(): jnp.dot(segments, this_table, preferred_element_type=jnp.float32)  45.7 us
    all_to_all x1, waiting for transfers between devices, on_device(): lax.all_to_all(raw_samples, 'wide', split_axis=1, concat_axis=0, tiled=True)  41.4 us
    all_to_all x1, waiting for transfers between devices, on_device(): lax.all_to_all(jnp.stack(lax.axis_size('narrow') * [whitened]), 'narrow',...  39.6 us
    gather x48, local copies, waits for them, and re-layouts  32.5 us
    another operation x1, local copies, waits for them, and re-layouts, decimate(): segments = samples.reshape(-1, DECIM * block_size)  13.5 us
  transfers between devices with their start and end apart: 3, of which 3 were waited for; matrix products, arithmetic and copies ran while one was open for 17% of the time, Pallas kernels for 0%

profile of v1, /device:TPU:0, one launch (start us, length us, event | category | flops | bytes accessed | tf_op | source)
XLA Modules:
  0.0 480.1 jit_solution(7911864843544485034)
XLA Ops:
  6.5 11.2 %copy.31 = bf16[8,32,16384]{2,0,1:T(8,128)(2,1)} copy(bf16[8,32,16384]{2,1,0:T(8,128)(2,1)} %param.6) | data formatting | bytes 16777216 | tf_op args[0]
  17.7 7.9 %all-to-all-start = ((bf16[8,32,16384]{2,0,1:T(8,128)(2,1)}), bf16[8,32,16384]{2,0,1:T(8,128)(2,1)}, u32[]{:S(2)}, u32[]{:S(2)}) async-start(bf16[8,32,16384]{2,0,1:T(8,128)(2,1)} %copy.31), calls=%async_computation | async-start | bytes 16777216 | tf_op jit(solution)/shard_map/all_to_all | solution.py:141
  25.8 0.7 fusion.579
  26.6 0.7 fusion.580
  27.3 0.7 fusion.581
  28.0 0.7 fusion.582
  28.7 69.1 %cosine_convert_fusion = (bf16[4096,1024]{1,0:T(8,128)(2,1)}, bf16[4096,1024]{1,0:T(8,128)(2,1)}) fusion(s32[1024]{0:T(1024)S(1)} %iota_add_fusion), kind=kLoop, calls=%fused_computation.15 | loop fusion | flops 71303168 | bytes 16781312 | tf_op jit(solution)/shard_map/convert.24
  97.8 41.4 %all-to-all-done = bf16[8,32,16384]{2,0,1:T(8,128)(2,1)} async-done(((bf16[8,32,16384]{2,0,1:T(8,128)(2,1)}), bf16[8,32,16384]{2,0,1:T(8,128)(2,1)}, u32[]{:S(2)}, u32[]{:S(2)}) %all-to-all-start) | async-done | bytes 8388640 | tf_op jit(solution)/shard_map/all_to_all | solution.py:141
  139.2 13.5 %reshape_reshape.3 = bf16[8192,512]{1,0:T(8,128)(2,1)} reshape(bf16[32,8,1,16384]{3,1,0,2:T(8,128)(2,1)} %bitcast.65) | data formatting | bytes 16777216 | tf_op jit(solution)/shard_map/reshape;reshape | solution.py:37
  152.6 50.2 %convolution_bitcast_fusion = f32[8192,128]{0,1:T(8,128)} fusion(bf16[8192,512]{1,0:T(8,128)(2,1)} %reshape_reshape.3, bf16[]{:T(256)} %bitcast.63, bf16[]{:T(256)} %bitcast.62, bf16[]{:T(256)} %bitcast.61, bf16[]{:T(256)} %bitcast.60, bf16[]{:T(256)} %bitcast.59, bf16[]{:T(256)} %bitcast.58, bf16[]{:T(256)} %bitcast.57, bf16[]{:T(256)} %bitcast.56, ...), kind=kOutput, calls=%fused_computation.19 | convolution fusion | flops 1082916864 | bytes 12583552 | tf_op jit(solution)/shard_map/dot_general | solution.py:41
  202.8 45.7 %convolution_bitcast_fusion.1 = f32[8192,128]{0,1:T(8,128)} fusion(bf16[8192,512]{1,0:T(8,128)(2,1)S(1)} %bitcast.200, bf16[]{:T(256)} %bitcast.63, bf16[]{:T(256)} %bitcast.62, bf16[]{:T(256)} %bitcast.61, bf16[]{:T(256)} %bitcast.60, bf16[]{:T(256)} %bitcast.59, bf16[]{:T(256)} %bitcast.58, bf16[]{:T(256)} %bitcast.57, bf16[]{:T(256)} %bitcast.56, ...), kind=kOutput, calls=%fused_computation.20 | convolution fusion | flops 1082851328 | bytes 12583552 | tf_op jit(solution)/shard_map/dot_general | solution.py:38
  248.5 5.6 %copy.33 = f32[8192,128]{1,0:T(8,128)} copy(f32[8192,128]{0,1:T(8,128)} %convolution_bitcast_fusion) | data formatting | bytes 8388608 | tf_op jit(solution)/shard_map/dot_general | solution.py:41
  254.1 5.6 %copy.32 = f32[8192,128]{1,0:T(8,128)} copy(f32[8192,128]{0,1:T(8,128)} %convolution_bitcast_fusion.1) | data formatting | bytes 8388608 | tf_op jit(solution)/shard_map/dot_general | solution.py:38
  259.7 4.2 add_convert_fusion
  263.9 2.7 copy.34
  266.6 10.9 %fusion.3 = f32[256,2048]{1,0:T(8,128)S(1)} fusion(bf16[256,4096]{0,1:T(8,128)(2,1)} %bitcast.203, bf16[4096,1024]{1,0:T(8,128)(2,1)} %get-tuple-element.47, bf16[4096,1024]{1,0:T(8,128)(2,1)} %get-tuple-element.46), kind=kOutput, calls=%fused_computation.10 | convolution fusion | flops 4328521728 | bytes 20971520 | tf_op jit(solution)/shard_map/dot_general | solution.py:74
  277.5 3.8 fusion.583
  281.9 2.5 stack.3
  284.5 5.4 %all-to-all-start.1 = ((bf16[4,256,1,2048]{3,1,2,0:T(8,128)(2,1)}), bf16[4,256,1,2048]{3,1,2,0:T(8,128)(2,1)}, u32[]{:S(2)}, u32[]{:S(2)}) async-start(bf16[4,256,1,2048]{3,1,2,0:T(8,128)(2,1)} %stack.3), calls=%async_computation.1 | async-start | bytes 8388608 | tf_op jit(solution)/shard_map/all_to_all | solution.py:158
  290.5 39.6 %all-to-all-done.1 = bf16[4,256,1,2048]{3,1,2,0:T(8,128)(2,1)} async-done(((bf16[4,256,1,2048]{3,1,2,0:T(8,128)(2,1)}), bf16[4,256,1,2048]{3,1,2,0:T(8,128)(2,1)}, u32[]{:S(2)}, u32[]{:S(2)}) %all-to-all-start.1) | async-done | bytes 4194336 | tf_op jit(solution)/shard_map/all_to_all | solution.py:158
  330.2 16.7 %while.2 = (s32[]{:T(128)}, bf16[1024,1,2048]{2,0,1:T(8,128)(2,1)}, s32[8,3]{0,1:T(4,128)S(1)}, bf16[8,8,1,2048]{3,1,2,0:T(8,128)(2,1)S(1)}, s32[]{:T(128)}) while((s32[]{:T(128)}, bf16[1024,1,2048]{2,0,1:T(8,128)(2,1)}, s32[8,3]{0,1:T(4,128)S(1)}, bf16[8,8,1,2048]{3,1,2,0:T(8,128)(2,1)S(1)}, s32[]{:T(128)}) %tuple.100), condition=%wide.while_cond, body=%wide.while_body.sunk | while | flops 2 | bytes 65641 | solution.py:97
  331.1 1.4 bitcast_dynamic-update-slice_fusion.4
  333.1 1.4 bitcast_dynamic-update-slice_fusion.4
  334.7 0.5 slice.413
  335.2 1.4 bitcast_dynamic-update-slice_fusion.4
  337.2 1.4 bitcast_dynamic-update-slice_fusion.4
  339.3 1.4 bitcast_dynamic-update-slice_fusion.4
  340.8 0.5 slice.413
  341.3 1.4 bitcast_dynamic-update-slice_fusion.4
  343.4 1.4 bitcast_dynamic-update-slice_fusion.4
  345.4 1.4 bitcast_dynamic-update-slice_fusion.4
  347.3 16.4 %while.3 = (s32[]{:T(128)}, bf16[1024,1,2048]{2,0,1:T(8,128)(2,1)}, s32[8,3]{0,1:T(4,128)S(1)}, bf16[8,8,1,2048]{3,1,2,0:T(8,128)(2,1)S(1)}, s32[]{:T(128)}) while((s32[]{:T(128)}, bf16[1024,1,2048]{2,0,1:T(8,128)(2,1)}, s32[8,3]{0,1:T(4,128)S(1)}, bf16[8,8,1,2048]{3,1,2,0:T(8,128)(2,1)S(1)}, s32[]{:T(128)}) %tuple.97), condition=%wide.while_cond.1, body=%wide.while_body.1.sunk | while | flops 2 | bytes 65641 | solution.py:97
  347.9 1.4 bitcast_dynamic-update-slice_fusion.5
  349.4 0.5 slice.414
  349.9 1.4 bitcast_dynamic-update-slice_fusion.5
  352.0 1.4 bitcast_dynamic-update-slice_fusion.5
  354.0 1.4 bitcast_dynamic-update-slice_fusion.5
  356.1 1.4 bitcast_dynamic-update-slice_fusion.5
  358.1 1.4 bitcast_dynamic-update-slice_fusion.5
  359.7 0.5 slice.414
  360.2 1.4 bitcast_dynamic-update-slice_fusion.5
  362.2 1.4 bitcast_dynamic-update-slice_fusion.5
  364.0 0.6 multiply_add_fusion
  364.6 2.6 maximum_multiply_fusion
  367.3 9.7 %cosine_multiply_fusion = (f32[1024,512]{1,0:T(8,128)S(1)}, f32[1024,512]{1,0:T(8,128)}) fusion(s32[512]{0:T(512)S(1)} %iota_add_fusion.1, s32[1024]{0:T(1024)S(1)} %iota_add_fusion), kind=kLoop, calls=%fused_computation.42 | loop fusion | flops 8912896 | bytes 4200448 | tf_op jit(solution)/shard_map/mul | solution.py:62
  377.0 91.8 %reduce-scatter.2.cloned.1.call-done = f32[2,8,2048]{2,1,0:T(8,128)} async-done(((f32[64,8,2048]{2,1,0:T(8,128)}), f32[2,8,2048]{2,1,0:T(8,128)}) %reduce-scatter.2.cloned.1.call-update) | async-done | bytes 131088 | tf_op jit(solution)/shard_map/reduce_scatter | solution.py:129
  468.8 3.8 fusion.20
  472.6 0.6 copy.39
  (67 shorter events, 9.6 us)
Async XLA Ops:
  17.7 8.1 %copy-start = (f32[64]{0:T(128)S(1)}, f32[64]{0:T(128)}, u32[]{:S(2)}) copy-start(f32[64]{0:T(128)} %param.7) | copy-start | bytes 772
  17.7 121.4 %all-to-all-start = ((bf16[8,32,16384]{2,0,1:T(8,128)(2,1)}), bf16[8,32,16384]{2,0,1:T(8,128)(2,1)}, u32[]{:S(2)}, u32[]{:S(2)}) async-start(bf16[8,32,16384]{2,0,1:T(8,128)(2,1)} %copy.31), calls=%async_computation | async-start | bytes 16777216 | tf_op jit(solution)/shard_map/all_to_all | solution.py:141
  152.6 50.2 %slice-start = ((s8[8388608]{0:T(1024)(128)(4,1)}), s8[4194304]{0:T(1024)(128)(4,1)S(1)}, s32[]{:S(2)}) async-start(s8[8388608]{0:T(1024)(128)(4,1)} %bitcast.199), calls=%async_computation.4 | async-start | bytes 8388608
  152.6 50.2 %slice-start.1 = ((s8[8388608]{0:T(1024)(128)(4,1)}), s8[4194304]{0:T(1024)(128)(4,1)S(1)}, s32[]{:S(2)}) async-start(s8[8388608]{0:T(1024)(128)(4,1)} %bitcast.199), calls=%async_computation.5 | async-start | bytes 8388608
  284.5 5.4 %copy-start.2 = (s32[16]{0:T(128)S(1)}, s32[16]{0:T(128)}, u32[]{:S(2)}) copy-start(s32[16]{0:T(128)} %param.9) | copy-start | bytes 196
  284.5 5.7 %copy-start.1 = (s32[16,2]{0,1:T(2,128)S(1)}, s32[16,2]{0,1:T(2,128)}, u32[]{:S(2)}) copy-start(s32[16,2]{0,1:T(2,128)} %param.8) | copy-start | bytes 388
  284.5 45.7 %all-to-all-start.1 = ((bf16[4,256,1,2048]{3,1,2,0:T(8,128)(2,1)}), bf16[4,256,1,2048]{3,1,2,0:T(8,128)(2,1)}, u32[]{:S(2)}, u32[]{:S(2)}) async-start(bf16[4,256,1,2048]{3,1,2,0:T(8,128)(2,1)} %stack.3), calls=%async_computation.1 | async-start | bytes 8388608 | tf_op jit(solution)/shard_map/all_to_all | solution.py:158
  289.9 178.9 %reduce-scatter.2.cloned.1.call-start = ((), (), s32[]{:S(2)}) async-start(), calls=%async_computation.3 | async-start | bytes 4325376 | tf_op jit(solution)/shard_map/reduce_scatter | solution.py:129
Sparse Core Ops, SparseCore 0:
  367.4 101.3 reduce-scatter.1
